TPU v7x, 256 devices: a whole 4x4x8 slice. The times are simulated.
256 devices in a mesh: section: 2 (over core), seq: 16 (over x, y), exp: 8 (over z).
Axes of the slice: x: 4, y: 4, z: 8, core: 2. Of those that a mesh axis runs over, the one named last changes fastest.
Arguments:
- hidden_in: bfloat16 [2048, 2048], P('seq'), may hold values from -6 to 6
- seg_ids: int32 [2048], P('seq'), may hold values from 0 to 7, never falling along the last dimension, each value on 1 to 1024 neighbouring positions
- attn_gain: float32 [2048], replicated, may hold values from 0.25 to 1.75
- w_query: bfloat16 [2048, 2048], P(None, ('section', 'exp'))
- w_key: bfloat16 [2048, 2048], P(None, ('section', 'exp'))
- w_value: bfloat16 [2048, 2048], P(None, ('section', 'exp')), may hold values from -0.125 to 0.125
- w_out: bfloat16 [2048, 2048], P(('section', 'exp')), may hold values from -0.5 to 0.5
- moe_gain: float32 [2048], replicated, may hold values from 0.25 to 1.75
- expert_ids: int32 [2048, 8], P(('seq', 'exp')), may hold values from 0 to 63, all different within a row; in each aligned block of 16 rows (0 to 15, 16 to 31, ...) at most 4 rows name the same one
- route_weights: float32 [2048, 8], P(('seq', 'exp')), may hold values from 0.1 to 0.6
- gate_halves: bfloat16 [128, 2048, 512], P(('seq', 'exp'), None, 'section'), may hold values from -0.125 to 0.125
- up_halves: bfloat16 [128, 2048, 512], P(('seq', 'exp'), None, 'section'), may hold values from -0.125 to 0.125
- down_halves: bfloat16 [128, 512, 2048], P(('seq', 'exp'), 'section'), may hold values from -0.1875 to 0.1875
Outputs:
- layer_out: bfloat16 [2048, 2048], P(('seq', 'exp'))
Inputs may be any that keep to these rules, and one draw needn't show every extreme that they name: `seg_ids`: prompt numbers never fall along the batch; each prompt holds 1 to 1024 tokens, and one holds exactly 1024. `expert_ids`: A token's 8 experts are distinct. In each aligned block of 16 tokens (the tokens of one device along seq and exp), no expert is chosen by more than 4 of the block's tokens, a bound that some block reaches.
All inputs are finite; a program needn't handle non-finite values.
Results may differ from a plain program's by a relative error of at most 0.012.
Values may be sent and summed in bfloat16 or wider, within the bound.
No kernel may reach another device: no remote copies, remote signals or barrier semaphores. Data moves between devices by JAX's collectives and lax.ppermute only.
A program may use at most 64 MiB of HBM per device.

v0:
```python
import math

import jax
import jax.numpy as jnp
from jax import lax
from jax.sharding import PartitionSpec as P

epsilon = 1e-05
rope_base = 10000.0


def rms_scale(rows, gain):
    wide = rows.astype(jnp.float32)
    inverse = lax.rsqrt(jnp.mean(wide * wide, axis=-1, keepdims=True) + epsilon)
    return (wide * inverse * gain).astype(jnp.bfloat16)


def rotate(values, positions):
    half_dim = values.shape[-1] // 2
    frequency = rope_base ** (-2.0 * jnp.arange(half_dim, dtype=jnp.float32) / values.shape[-1])
    angles = positions.astype(jnp.float32)[:, None] * frequency[None, :]
    cosine = jnp.cos(angles)
    sine_part = jnp.sin(angles)
    first_half = values[:, :half_dim]
    second_half = values[:, half_dim:]
    return jnp.concatenate(
        [
            first_half * cosine - second_half * sine_part,
            second_half * cosine + first_half * sine_part,
        ],
        axis=-1,
    )


def per_device(
    hidden_in,
    seg_ids,
    attn_gain,
    w_query,
    w_key,
    w_value,
    w_out,
    moe_gain,
    expert_ids,
    route_weights,
    gate_halves,
    up_halves,
    down_halves,
):
    tok_seq = hidden_in.shape[0]
    width = hidden_in.shape[1]
    head_dim = w_query.shape[1]
    positions = lax.axis_index("seq") * tok_seq + jnp.arange(tok_seq, dtype=jnp.int32)
    normed = rms_scale(hidden_in, attn_gain)
    query_rows = rotate(
        jnp.dot(normed, w_query, preferred_element_type=jnp.float32), positions
    ).astype(jnp.bfloat16)
    key_rows = rotate(jnp.dot(normed, w_key, preferred_element_type=jnp.float32), positions).astype(
        jnp.bfloat16
    )
    value_rows = jnp.dot(normed, w_value, preferred_element_type=jnp.float32).astype(jnp.bfloat16)
    score_scale = 1.0 / math.sqrt(head_dim)
    run_max = jnp.full((tok_seq,), -1e30, jnp.float32)
    piece_keys = lax.all_gather(key_rows, "seq", axis=0, tiled=True)
    piece_values = lax.all_gather(value_rows, "seq", axis=0, tiled=True)
    key_segs = lax.all_gather(seg_ids, "seq", axis=0, tiled=True)
    piece_rows = piece_keys.shape[0]
    scores = (
        lax.dot_general(
            query_rows, piece_keys, (((1,), (1,)), ((), ())), preferred_element_type=jnp.float32
        )
        * score_scale
    )
    key_pos = jnp.arange(piece_rows, dtype=jnp.int32)
    allowed = (seg_ids[:, None] == key_segs[None, :]) & (key_pos[None, :] <= positions[:, None])
    masked = jnp.where(allowed, scores, -1e30)
    new_max = jnp.maximum(run_max, jnp.max(masked, axis=1))
    weights = jnp.where(allowed, jnp.exp(masked - new_max[:, None]), 0.0)
    run_total = jnp.sum(weights, axis=1)
    weighted_sum = jnp.dot(
        weights.astype(jnp.bfloat16), piece_values, preferred_element_type=jnp.float32
    )
    run_max, run_total, weighted_sum = (new_max, run_total, weighted_sum)
    head_out = (weighted_sum / run_total[:, None]).astype(jnp.bfloat16)
    partial_value = jnp.dot(head_out, w_out, preferred_element_type=jnp.float32)
    tok_dev = tok_seq // lax.axis_size("exp")
    own_start = lax.axis_index("exp") * tok_dev
    summed = lax.psum(partial_value, ("section", "exp"))
    summed = lax.dynamic_slice_in_dim(summed, own_start, tok_dev, 0)
    own_rows = lax.dynamic_slice_in_dim(hidden_in, own_start, tok_dev, 0)
    residual = (own_rows.astype(jnp.float32) + summed).astype(jnp.bfloat16)
    moe_in = rms_scale(residual, moe_gain)
    experts = lax.axis_size("seq") * lax.axis_size("exp") // 2
    top_count = expert_ids.shape[1]
    capacity = min(tok_dev, max(2, 2 * tok_dev * top_count // experts))
    row_count = tok_dev * top_count
    flat_ids = expert_ids.reshape(row_count)
    one_hot = (flat_ids[:, None] == jnp.arange(experts, dtype=jnp.int32)[None, :]).astype(jnp.int32)
    slot_rank = jnp.sum((jnp.cumsum(one_hot, axis=0) - one_hot) * one_hot, axis=1)
    slot_index = flat_ids * capacity + slot_rank
    placed = slot_index[:, None] == jnp.arange(experts * capacity, dtype=jnp.int32)[None, :]
    repeated = jnp.repeat(moe_in, top_count, axis=0)
    outgoing = lax.dot_general(
        placed.astype(jnp.bfloat16),
        repeated,
        (((0,), (0,)), ((), ())),
        preferred_element_type=jnp.float32,
    ).astype(jnp.bfloat16)
    row_token = jnp.arange(row_count, dtype=jnp.int32) // top_count
    token_hot = (row_token[None, :] == jnp.arange(tok_dev, dtype=jnp.int32)[:, None]).astype(
        jnp.float32
    )
    weighted = token_hot * route_weights.reshape(row_count)[None, :]
    combine = jnp.dot(weighted, placed.astype(jnp.float32), precision=lax.Precision.HIGHEST)
    doubled = jnp.broadcast_to(
        outgoing.reshape(experts, 1, capacity, width), (experts, 2, capacity, width)
    ).reshape(2 * experts, capacity, width)
    arrived = lax.all_to_all(doubled, ("seq", "exp"), split_axis=0, concat_axis=0, tiled=True)
    flat_rows = arrived.reshape(-1, width)
    gate_proj = jnp.dot(flat_rows, gate_halves[0], preferred_element_type=jnp.float32)
    up_proj = jnp.dot(flat_rows, up_halves[0], preferred_element_type=jnp.float32)
    activated = (jax.nn.silu(gate_proj) * up_proj).astype(jnp.bfloat16)
    returned = lax.all_to_all(
        jnp.dot(activated, down_halves[0], preferred_element_type=jnp.float32)
        .astype(jnp.bfloat16)
        .reshape(arrived.shape),
        ("seq", "exp"),
        split_axis=0,
        concat_axis=0,
        tiled=True,
    )
    halves_sum = jnp.sum(
        returned.reshape(experts, 2, capacity, width).astype(jnp.float32), axis=1
    ).reshape(experts * capacity, width)
    moe_part = jnp.dot(combine, halves_sum, precision=lax.Precision.HIGHEST)
    moe_total = lax.psum(moe_part, "section")
    return (residual.astype(jnp.float32) + moe_total).astype(jnp.bfloat16)


def solution(mesh):
    in_specs = (
        P("seq", None),
        P("seq"),
        P(),
        P(None, ("section", "exp")),
        P(None, ("section", "exp")),
        P(None, ("section", "exp")),
        P(("section", "exp"), None),
        P(),
        P(("seq", "exp"), None),
        P(("seq", "exp"), None),
        P(("seq", "exp"), None, "section"),
        P(("seq", "exp"), None, "section"),
        P(("seq", "exp"), "section", None),
    )
    out_specs = P(("seq", "exp"), None)
    return jax.shard_map(
        per_device, mesh=mesh, in_specs=in_specs, out_specs=out_specs, check_vma=False
    )
```

profile of v0, /device:TPU:1, one launch (start us, length us, event | category | flops | bytes accessed | tf_op | source)
XLA Modules:
  0.0 376.0 jit_solution(10940934380651629049)
XLA Ops:
  6.5 0.0 copy-start
  6.5 0.0 copy-start.4
  6.5 0.0 all-reduce.3.cloned.1.call-start
  6.6 1.3 fusion.4
  7.9 1.6 fusion.74
  9.5 0.0 copy-start.2
  9.5 0.0 copy-start.7
  9.6 0.0 copy-start.8
  9.6 1.7 fusion.76
  11.3 0.2 fusion.52
  11.5 20.5 %all_gather.10 = bf16[2048,128]{0,1:T(8,128)(2,1)S(1)} all-gather(bf16[128,128]{0,1:T(8,128)(2,1)S(1)} %pad_maximum_fusion), channel_id=1, replica_groups=mesh['section'=2,'seq'=16,'exp'=8] {'seq'}, dimensions={0}, use_global_device_ids=true | all-gather | bytes 557056 | tf_op jit(solution)/shard_map/all_gather | solution.py:64
  32.0 0.0 copy-done.4
  32.0 15.7 %all-gather = s32[16,1,128]{2,1,0:T(1,128)S(1)} all-gather(s32[1,1,128]{2,1,0:T(1,128)S(1)} %bitcast.33), channel_id=1, replica_groups=mesh['section'=2,'seq'=16,'exp'=8] {'seq'}, dimensions={0}, use_global_device_ids=true | all-gather | bytes 8704 | tf_op jit(solution)/shard_map/all_gather | solution.py:66
  47.8 0.5 fusion.78
  48.3 0.0 copy-done.2
  48.3 0.0 copy-done.7
  48.3 0.0 copy-done.8
  48.3 0.4 convolution_convert_fusion.2
  48.7 16.1 %all_gather.11 = bf16[2048,128]{1,0:T(8,128)(2,1)S(1)} all-gather(bf16[128,128]{1,0:T(8,128)(2,1)S(1)} %convolution_convert_fusion.2), channel_id=1, replica_groups=mesh['section'=2,'seq'=16,'exp'=8] {'seq'}, dimensions={0}, use_global_device_ids=true | all-gather | bytes 557056 | tf_op jit(solution)/shard_map/all_gather | solution.py:65
  64.8 0.4 fusion.13
  65.2 0.0 copy-start.5
  65.2 0.0 copy-start.3
  65.2 2.8 fusion.3
  68.0 0.0 all-reduce.3.cloned.1.call-update
  68.1 0.0 copy-done.5
  68.1 0.1 copy.19
  68.1 0.1 reshape.82
  68.2 0.1 fusion.42
  68.3 0.2 reduce_window_sum.11
  68.5 0.2 select_reduce_fusion
  68.7 128.0 %all-reduce.3.cloned.1.call-done = f32[128,2048]{1,0:T(8,128)} async-done(((f32[128,2048]{1,0:T(8,128)}), f32[128,2048]{1,0:T(8,128)}) %all-reduce.3.cloned.1.call-update) | async-done | bytes 1048592 | tf_op jit(solution)/shard_map/psum | solution.py:88
  196.7 1.0 fusion.35
  197.7 0.0 copy-done.3
  197.7 0.1 fusion.37
  197.8 0.5 convolution_convert_fusion.1
  198.4 0.4 broadcast_in_dim.19
  198.8 1.2 broadcast_in_dim.20
  200.1 63.0 %all_to_all.10 = bf16[128,4,2048]{2,1,0:T(4,128)(2,1)S(1)} all-to-all(bf16[128,4,2048]{2,1,0:T(4,128)(2,1)S(1)} %bitcast.29), channel_id=1, replica_groups=mesh['section'=2,'seq'=16,'exp'=8] {'seq','exp'}, dimensions={0} | all-to-all | bytes 4194304 | tf_op jit(solution)/shard_map/all_to_all | solution.py:118
  263.1 2.1 reshape.85
  265.1 0.0 copy-start.1
  265.1 3.5 fusion.10
  268.7 0.0 copy-done
  268.7 0.0 copy-done.1
  268.7 5.0 %convolution_convert_fusion = bf16[512,2048]{1,0:T(8,128)(2,1)} fusion(bf16[512,2048]{1,0:T(8,128)(2,1)S(1)} %copy-done.1, bf16[1,256,2048]{2,1,0:T(8,128)(2,1)S(1)} %copy-done, bf16[1,2048,256]{2,1,0:T(8,128)(2,1)} %param.24, f32[512,256]{1,0:T(8,128)} %fusion.10), kind=kOutput, calls=%fused_computation.1 | convolution fusion | flops 1075576832 | bytes 6815744 | tf_op jit(solution)/shard_map/dot_general | solution.py:124
  273.7 4.1 %reshape.86 = bf16[128,4,2048]{2,1,0:T(4,128)(2,1)} reshape(bf16[512,2048]{1,0:T(8,128)(2,1)} %convolution_convert_fusion) | data formatting | bytes 4194304 | tf_op jit(solution)/shard_map/reshape | solution.py:126
  277.8 0.0 copy-start.6
  277.8 6.7 %all-to-all-start.1 = ((bf16[128,4,2048]{2,1,0:T(4,128)(2,1)}), bf16[128,4,2048]{2,1,0:T(4,128)(2,1)S(1)}, u32[]{:S(2)}, u32[]{:S(2)}) async-start(bf16[128,4,2048]{2,1,0:T(4,128)(2,1)} %reshape.86), calls=%async_computation.1 | async-start | bytes 4194304 | tf_op jit(solution)/shard_map/all_to_all | solution.py:123
  284.6 0.2 all-reduce.5.cloned.1.call-start
  284.8 0.0 copy-done.6
  284.8 0.1 copy.18
  284.9 0.1 mul.147
  285.0 0.2 fusion.39
  285.2 49.4 %all-to-all-done.1 = bf16[128,4,2048]{2,1,0:T(4,128)(2,1)S(1)} async-done(((bf16[128,4,2048]{2,1,0:T(4,128)(2,1)}), bf16[128,4,2048]{2,1,0:T(4,128)(2,1)S(1)}, u32[]{:S(2)}, u32[]{:S(2)}) %all-to-all-start.1) | async-done | bytes 2097184 | tf_op jit(solution)/shard_map/all_to_all | solution.py:123
  334.5 2.7 convert_reduce_fusion
  337.2 2.0 reshape.87
  339.2 1.8 fusion.79
  341.0 0.0 all-reduce.5.cloned.1.call-update
  341.0 26.6 %all-reduce.5.cloned.1.call-done = f32[16,2048]{1,0:T(8,128)} async-done(((f32[16,2048]{1,0:T(8,128)}), f32[16,2048]{1,0:T(8,128)}) %all-reduce.5.cloned.1.call-update) | async-done | bytes 131088 | tf_op jit(solution)/shard_map/psum | solution.py:136
  367.6 1.5 fusion.38
  (9 shorter events, 0.1 us)
Async XLA Ops:
  6.5 262.1 %copy-start = (bf16[1,256,2048]{2,1,0:T(8,128)(2,1)S(1)}, bf16[1,256,2048]{2,1,0:T(8,128)(2,1)}, u32[]{:S(2)}) copy-start(bf16[1,256,2048]{2,1,0:T(8,128)(2,1)} %param.25) | copy-start | bytes 3145732
  6.5 25.5 %copy-start.4 = (s32[128]{0:T(128)S(1)}, s32[128]{0:T(128)}, u32[]{:S(2)}) copy-start(s32[128]{0:T(128)} %param.14) | copy-start | bytes 1540
  6.5 190.1 %all-reduce.3.cloned.1.call-start = ((), (), s32[]{:S(2)}) async-start(), calls=%async_computation.2 | async-start | bytes 2097152 | tf_op jit(solution)/shard_map/psum | solution.py:88
  9.5 38.8 %copy-start.2 = (bf16[128,2048]{1,0:T(8,128)(2,1)S(1)}, bf16[128,2048]{1,0:T(8,128)(2,1)}, u32[]{:S(2)}) copy-start(bf16[128,2048]{1,0:T(8,128)(2,1)} %param.13) | copy-start | bytes 1572868
  9.5 38.8 %copy-start.7 = (bf16[2048,128]{1,0:T(8,128)(2,1)S(1)}, bf16[2048,128]{1,0:T(8,128)(2,1)}, u32[]{:S(2)}) copy-start(bf16[2048,128]{1,0:T(8,128)(2,1)} %param.18) | copy-start | bytes 1572868
  9.6 38.8 %copy-start.8 = (f32[2048]{0:T(1024)S(1)}, f32[2048]{0:T(1024)}, u32[]{:S(2)}) copy-start(f32[2048]{0:T(1024)} %param.15) | copy-start | bytes 24580
  65.2 2.8 copy-start.5
  65.2 132.5 %copy-start.3 = (f32[2048]{0:T(1024)S(1)}, f32[2048]{0:T(1024)}, u32[]{:S(2)}) copy-start(f32[2048]{0:T(1024)} %param.20) | copy-start | bytes 24580
  265.1 3.5 copy-start.1
  277.8 7.0 %copy-start.6 = (f32[16,8]{0,1:T(8,128)S(1)}, f32[16,8]{0,1:T(8,128)}, u32[]{:S(2)}) copy-start(f32[16,8]{0,1:T(8,128)} %param.22) | copy-start | bytes 1540
  277.8 56.7 %all-to-all-start.1 = ((bf16[128,4,2048]{2,1,0:T(4,128)(2,1)}), bf16[128,4,2048]{2,1,0:T(4,128)(2,1)S(1)}, u32[]{:S(2)}, u32[]{:S(2)}) async-start(bf16[128,4,2048]{2,1,0:T(4,128)(2,1)} %reshape.86), calls=%async_computation.1 | async-start | bytes 4194304 | tf_op jit(solution)/shard_map/all_to_all | solution.py:123
  284.6 83.1 %all-reduce.5.cloned.1.call-start = ((), (), s32[]{:S(2)}) async-start(), calls=%async_computation.3 | async-start | bytes 262144 | tf_op jit(solution)/shard_map/psum | solution.py:136
Sparse Core Ops, SparseCore 0:
  68.2 128.4 all-reduce.2
  341.1 26.4 all-reduce.4
where the time goes:
time: 377 us; the launch traced here: 376 us
  waiting for transfers between devices  204 us (54%)
  blocking collectives  115 us (31%)
  matrix products  18 us (5%)
  between operations  13.6 us (4%)
  local copies, waits for them, and re-layouts  10.2 us (3%)
  other arithmetic  7.82 us (2%)
  starting transfers between devices  6.96 us (2%)
    psum x1, waiting for transfers between devices, per_device(): summed = lax.psum(partial_value, ('section', 'exp'))  128 us
    all_to_all x1, blocking collectives, per_device(): lax.all_to_all(doubled, ('seq', 'exp'), split_axis=0, concat_axis=0, tile...  63 us
    all_to_all x1, waiting for transfers between devices, per_device(): lax.all_to_all(jnp.dot(activated, down_halves[0], preferred_element_type=...  49.4 us
    psum x1, waiting for transfers between devices, per_device(): moe_total = lax.psum(moe_part, 'section')  26.6 us
    all_gather x1, blocking collectives, per_device(): piece_keys = lax.all_gather(key_rows, 'seq', axis=0, tiled=True)  20.5 us
    all_gather x1, blocking collectives, per_device(): piece_values = lax.all_gather(value_rows, 'seq', axis=0, tiled=True)  16.1 us
    all_gather x1, blocking collectives, per_device(): key_segs = lax.all_gather(seg_ids, 'seq', axis=0, tiled=True)  15.7 us
  transfers between devices with their start and end apart: 3, of which 3 were waited for; matrix products, arithmetic and copies ran while one was open for 0% of the time, Pallas kernels for 0%

commit v1 on v0

--- a/solution.py
+++ b/solution.py
@@ -61,9 +61,12 @@
     value_rows = jnp.dot(normed, w_value, preferred_element_type=jnp.float32).astype(jnp.bfloat16)
     score_scale = 1.0 / math.sqrt(head_dim)
     run_max = jnp.full((tok_seq,), -1e30, jnp.float32)
-    piece_keys = lax.all_gather(key_rows, "seq", axis=0, tiled=True)
-    piece_values = lax.all_gather(value_rows, "seq", axis=0, tiled=True)
-    key_segs = lax.all_gather(seg_ids, "seq", axis=0, tiled=True)
+    seg_block = jnp.broadcast_to(seg_ids.astype(jnp.bfloat16)[:, None], (tok_seq, head_dim))
+    packed = jnp.concatenate([key_rows, value_rows, seg_block], axis=1)
+    gathered = lax.all_gather(packed, "seq", axis=0, tiled=True)
+    piece_keys = gathered[:, :head_dim]
+    piece_values = gathered[:, head_dim : 2 * head_dim]
+    key_segs = gathered[:, 2 * head_dim].astype(jnp.int32)
     piece_rows = piece_keys.shape[0]
     scores = (
         lax.dot_general(
@@ -85,8 +88,8 @@
     partial_value = jnp.dot(head_out, w_out, preferred_element_type=jnp.float32)
     tok_dev = tok_seq // lax.axis_size("exp")
     own_start = lax.axis_index("exp") * tok_dev
-    summed = lax.psum(partial_value, ("section", "exp"))
-    summed = lax.dynamic_slice_in_dim(summed, own_start, tok_dev, 0)
+    summed = lax.psum_scatter(partial_value, "exp", scatter_dimension=0, tiled=True)
+    summed = summed + lax.ppermute(summed, "section", [(0, 1), (1, 0)])
     own_rows = lax.dynamic_slice_in_dim(hidden_in, own_start, tok_dev, 0)
     residual = (own_rows.astype(jnp.float32) + summed).astype(jnp.bfloat16)
     moe_in = rms_scale(residual, moe_gain)
@@ -133,7 +136,7 @@
         returned.reshape(experts, 2, capacity, width).astype(jnp.float32), axis=1
     ).reshape(experts * capacity, width)
     moe_part = jnp.dot(combine, halves_sum, precision=lax.Precision.HIGHEST)
-    moe_total = lax.psum(moe_part, "section")
+    moe_total = moe_part + lax.ppermute(moe_part, "section", [(0, 1), (1, 0)])
     return (residual.astype(jnp.float32) + moe_total).astype(jnp.bfloat16)
 
 

time: 377 us -> 271 us (0.72)
  waiting for transfers between devices: 204 us -> 140 us
  blocking collectives: 115 us -> 63.8 us
  starting transfers between devices: 6.96 us -> 16 us
    psum x2 -> x0, waiting for transfers between devices: 155 us -> none  [the longest x1 128 us: per_device(): summed = lax.psum(partial_value, ('section', 'exp'))]
    all_gather x3 -> x0, blocking collectives: 52.4 us -> none  [the longest x1 20.5 us: per_device(): piece_keys = lax.all_gather(key_rows, 'seq', axis=0, tiled=True)]
    all_gather x0 -> x1, waiting for transfers between devices: none -> 52.2 us  [per_device(): gathered = lax.all_gather(packed, 'seq', axis=0, tiled=True)]
    reduce_scatter x0 -> x1, waiting for transfers between devices: none -> 35.1 us  [per_device(): lax.psum_scatter(partial_value, 'exp', scatter_dimension=0, tiled=True)]
    ppermute x0 -> x2, starting transfers between devices: none -> 9.37 us  [the longest x1 5.19 us: per_device(): summed = summed + lax.ppermute(summed, 'section', [(0, 1), (1, 0)])]
  transfers between devices with their start and end apart: 3 -> 5, of which waited for: 3 -> 5; matrix products, arithmetic and copies ran while one was open for 0% -> 0% of each run, Pallas kernels for 0% -> 0%
where the time goes in v1:
time: 271 us
  waiting for transfers between devices  140 us (52%)
  blocking collectives  63.8 us (24%)
  matrix products  18.4 us (7%)
  starting transfers between devices  16 us (6%)
  between operations  13.7 us (5%)
  local copies, waits for them, and re-layouts  10.2 us (4%)
  other arithmetic  8.38 us (3%)
    all_to_all x1, blocking collectives, per_device(): lax.all_to_all(doubled, ('seq', 'exp'), split_axis=0, concat_axis=0, tile...  63.8 us
    all_gather x1, waiting for transfers between devices, per_device(): gathered = lax.all_gather(packed, 'seq', axis=0, tiled=True)  52.2 us
    all_to_all x1, waiting for transfers between devices, per_device(): lax.all_to_all(jnp.dot(activated, down_halves[0], preferred_element_type=...  50.7 us
    reduce_scatter x1, waiting for transfers between devices, per_device(): lax.psum_scatter(partial_value, 'exp', scatter_dimension=0, tiled=True)  35.1 us
    all_to_all x1, starting transfers between devices, per_device(): lax.all_to_all(jnp.dot(activated, down_halves[0], preferred_element_type=...  6.52 us
  transfers between devices with their start and end apart: 5, of which 5 were waited for; matrix products, arithmetic and copies ran while one was open for 0% of the time, Pallas kernels for 0%

profile of v1, /device:TPU:1, one launch (start us, length us, event | category | flops | bytes accessed | tf_op | source)
XLA Modules:
  0.0 270.6 jit_solution(9258952518360087763)
XLA Ops:
  6.5 0.0 copy-start
  6.5 0.0 copy-start.2
  6.5 0.0 copy-start.9
  6.5 0.0 copy-start.8
  6.5 0.0 all-gather.2.cloned.1.call-start
  6.6 0.0 copy-start.7
  6.6 1.4 fusion.4
  8.0 1.6 fusion.76
  9.6 1.6 fusion.79
  11.3 0.0 copy-done.2
  11.3 0.0 copy-done.9
  11.3 0.0 copy-done.8
  11.3 0.4 convolution_convert_fusion.2
  11.7 0.0 copy-done.7
  11.7 0.0 copy-start.3
  11.7 0.2 fusion.59
  12.0 0.6 pad_maximum_fusion
  12.6 0.0 all-gather.2.cloned.1.call-update
  12.6 0.0 reduce-scatter.2.cloned.1.call-start
  12.7 52.2 %all-gather.2.cloned.1.call-done = bf16[2048,384]{0,1:T(8,128)(2,1)} async-done(((bf16[128,384]{0,1:T(8,128)(2,1)}), bf16[2048,384]{0,1:T(8,128)(2,1)}) %all-gather.2.cloned.1.call-update) | async-done | bytes 1572880 | tf_op jit(solution)/shard_map/all_gather | solution.py:66
  64.9 0.8 slice_convert_fusion
  65.7 1.5 fusion.81
  67.2 0.5 fusion.13
  67.7 0.0 copy-done.3
  67.7 0.0 copy-start.5
  67.7 0.0 copy-start.4
  67.7 2.8 %fusion.3 = f32[128,2048]{1,0:T(8,128)} fusion(bf16[128,2048]{1,0:T(8,128)(2,1)S(1)} %copy-done.3, f32[128,2048]{1,0:T(8,128)S(1)} %get-tuple-element.14, bf16[2048,384]{0,1:T(8,128)(2,1)} %all-gather.2.cloned.1.call-done, f32[128]{0:T(128)S(1)} %broadcast_maximum_fusion, s32[128]{0:T(128)S(1)} %iota_add_fusion, s32[2048]{0:T(1024)S(1)} %bitcast.29, ...), kind=kOutput, calls=%fused_computation.12 | convolution fusion | flops 135823360 | bytes 3155968 | tf_op jit(solution)/shard_map/dot_general | solution.py:88
  70.6 0.0 reduce-scatter.2.cloned.1.call-update
  70.6 0.0 copy-done.5
  70.6 0.1 copy.17
  70.7 0.1 reshape.89
  70.8 0.1 fusion.45
  70.9 0.2 reduce_window_sum.11
  71.0 0.2 select_reduce_fusion
  71.2 35.1 %reduce-scatter.2.cloned.1.call-done = f32[16,2048]{1,0:T(8,128)} async-done(((f32[128,2048]{1,0:T(8,128)}), f32[16,2048]{1,0:T(8,128)}) %reduce-scatter.2.cloned.1.call-update) | async-done | bytes 131088 | tf_op jit(solution)/shard_map/reduce_scatter | solution.py:91
  106.3 5.2 %collective-permute-start = (f32[16,2048]{1,0:T(8,128)}, f32[16,2048]{1,0:T(8,128)S(1)}, u32[]{:S(2)}, u32[]{:S(2)}) collective-permute-start(f32[16,2048]{1,0:T(8,128)} %reduce-scatter.2.cloned.1.call-done), channel_id=1, source_target_pairs={{0,128},{128,0},{1,129},{129,1},{2,130},{130,2},{3,131},{131,3},{4... | collective-permute-start | bytes 393224 | tf_op jit(solution)/shard_map/ppermute | solution.py:92
  111.5 1.2 collective-permute-done
  112.7 1.0 fusion.38
  113.7 0.0 copy-done.4
  113.7 0.1 fusion.40
  113.8 0.5 convolution_convert_fusion.1
  114.4 0.4 broadcast_in_dim.22
  114.8 1.2 broadcast_in_dim.23
  116.0 63.8 %all_to_all.10 = bf16[128,4,2048]{2,1,0:T(4,128)(2,1)S(1)} all-to-all(bf16[128,4,2048]{2,1,0:T(4,128)(2,1)S(1)} %bitcast.26), channel_id=1, replica_groups=mesh['section'=2,'seq'=16,'exp'=8] {'seq','exp'}, dimensions={0} | all-to-all | bytes 4194304 | tf_op jit(solution)/shard_map/all_to_all | solution.py:121
  179.9 2.1 reshape.92
  181.9 0.0 copy-start.1
  181.9 3.5 %fusion.10 = f32[512,256]{1,0:T(8,128)} fusion(bf16[512,2048]{1,0:T(8,128)(2,1)} %reshape.92, bf16[1,2048,256]{2,1,0:T(8,128)(2,1)} %param.23), kind=kOutput, calls=%fused_computation.18 | convolution fusion | flops 536870912 | bytes 3670016 | tf_op jit(solution)/shard_map/dot_general | solution.py:123
  185.5 0.0 copy-done
  185.5 0.0 copy-done.1
  185.5 5.0 %convolution_convert_fusion = bf16[512,2048]{1,0:T(8,128)(2,1)} fusion(bf16[512,2048]{1,0:T(8,128)(2,1)S(1)} %copy-done.1, bf16[1,256,2048]{2,1,0:T(8,128)(2,1)S(1)} %copy-done, bf16[1,2048,256]{2,1,0:T(8,128)(2,1)} %param.24, f32[512,256]{1,0:T(8,128)} %fusion.10), kind=kOutput, calls=%fused_computation.1 | convolution fusion | flops 1075576832 | bytes 6815744 | tf_op jit(solution)/shard_map/dot_general | solution.py:127
  190.5 4.1 %reshape.93 = bf16[128,4,2048]{2,1,0:T(4,128)(2,1)} reshape(bf16[512,2048]{1,0:T(8,128)(2,1)} %convolution_convert_fusion) | data formatting | bytes 4194304 | tf_op jit(solution)/shard_map/reshape | solution.py:129
  194.6 0.0 copy-start.6
  194.6 6.5 %all-to-all-start.1 = ((bf16[128,4,2048]{2,1,0:T(4,128)(2,1)}), bf16[128,4,2048]{2,1,0:T(4,128)(2,1)S(1)}, u32[]{:S(2)}, u32[]{:S(2)}) async-start(bf16[128,4,2048]{2,1,0:T(4,128)(2,1)} %reshape.93), calls=%async_computation.2 | async-start | bytes 4194304 | tf_op jit(solution)/shard_map/all_to_all | solution.py:126
  201.1 0.0 copy-done.6
  201.1 0.1 copy.16
  201.2 0.1 mul.147
  201.3 0.2 fusion.42
  201.5 50.7 %all-to-all-done.1 = bf16[128,4,2048]{2,1,0:T(4,128)(2,1)S(1)} async-done(((bf16[128,4,2048]{2,1,0:T(4,128)(2,1)}), bf16[128,4,2048]{2,1,0:T(4,128)(2,1)S(1)}, u32[]{:S(2)}, u32[]{:S(2)}) %all-to-all-start.1) | async-done | bytes 2097184 | tf_op jit(solution)/shard_map/all_to_all | solution.py:126
  252.2 2.7 convert_reduce_fusion
  254.9 2.0 reshape.94
  256.8 1.1 fusion.82
  257.9 4.2 %collective-permute-start.1 = (f32[16,2048]{1,0:T(8,128)S(1)}, f32[16,2048]{1,0:T(8,128)S(1)}, u32[]{:S(2)}, u32[]{:S(2)}) collective-permute-start(f32[16,2048]{1,0:T(8,128)S(1)} %fusion.82), channel_id=1, source_target_pairs={{0,128},{128,0},{1,129},{129,1},{2,130},{130,2},{3,131},{131,3},{4... | collective-permute-start | bytes 393224 | tf_op jit(solution)/shard_map/ppermute | solution.py:139
  262.1 1.0 collective-permute-done.1
  263.1 0.7 fusion.41
  (10 shorter events, 0.1 us)
Async XLA Ops:
  6.5 178.9 %copy-start = (bf16[1,256,2048]{2,1,0:T(8,128)(2,1)S(1)}, bf16[1,256,2048]{2,1,0:T(8,128)(2,1)}, u32[]{:S(2)}) copy-start(bf16[1,256,2048]{2,1,0:T(8,128)(2,1)} %param.25) | copy-start | bytes 3145732
  6.5 4.7 %copy-start.2 = (bf16[128,2048]{1,0:T(8,128)(2,1)S(1)}, bf16[128,2048]{1,0:T(8,128)(2,1)}, u32[]{:S(2)}) copy-start(bf16[128,2048]{1,0:T(8,128)(2,1)} %param.13) | copy-start | bytes 1572868
  6.5 4.7 %copy-start.9 = (f32[2048]{0:T(1024)S(1)}, f32[2048]{0:T(1024)}, u32[]{:S(2)}) copy-start(f32[2048]{0:T(1024)} %param.15) | copy-start | bytes 24580
  6.5 4.7 %copy-start.8 = (bf16[2048,128]{1,0:T(8,128)(2,1)S(1)}, bf16[2048,128]{1,0:T(8,128)(2,1)}, u32[]{:S(2)}) copy-start(bf16[2048,128]{1,0:T(8,128)(2,1)} %param.18) | copy-start | bytes 1572868
  6.5 58.4 %all-gather.2.cloned.1.call-start = ((), (), s32[]{:S(2)}) async-start(), calls=%async_computation.3 | async-start | bytes 1671168 | tf_op jit(solution)/shard_map/all_gather | solution.py:66
  6.6 5.1 %copy-start.7 = (s32[128]{0:T(128)S(1)}, s32[128]{0:T(128)}, u32[]{:S(2)}) copy-start(s32[128]{0:T(128)} %param.14) | copy-start | bytes 1540
  11.7 56.0 %copy-start.3 = (bf16[128,2048]{1,0:T(8,128)(2,1)S(1)}, bf16[128,2048]{1,0:T(8,128)(2,1)}, u32[]{:S(2)}) copy-start(bf16[128,2048]{1,0:T(8,128)(2,1)} %param.19) | copy-start | bytes 1572868
  12.6 93.7 %reduce-scatter.2.cloned.1.call-start = ((), (), s32[]{:S(2)}) async-start(), calls=%async_computation.4 | async-start | bytes 1179648 | tf_op jit(solution)/shard_map/reduce_scatter | solution.py:91
  67.7 2.9 %copy-start.5 = (s32[16,8]{0,1:T(8,128)S(1)}, s32[16,8]{0,1:T(8,128)}, u32[]{:S(2)}) copy-start(s32[16,8]{0,1:T(8,128)} %param.21) | copy-start | bytes 1540
  67.7 46.0 %copy-start.4 = (f32[2048]{0:T(1024)S(1)}, f32[2048]{0:T(1024)}, u32[]{:S(2)}) copy-start(f32[2048]{0:T(1024)} %param.20) | copy-start | bytes 24580
  106.3 6.4 %collective-permute-start = (f32[16,2048]{1,0:T(8,128)}, f32[16,2048]{1,0:T(8,128)S(1)}, u32[]{:S(2)}, u32[]{:S(2)}) collective-permute-start(f32[16,2048]{1,0:T(8,128)} %reduce-scatter.2.cloned.1.call-done), channel_id=1, source_target_pairs={{0,128},{128,0},{1,129},{129,1},{2,130},{130,2},{3,131},{131,3},{4... | collective-permute-start | bytes 393224 | tf_op jit(solution)/shard_map/ppermute | solution.py:92
  181.9 3.5 %copy-start.1 = (bf16[512,2048]{1,0:T(8,128)(2,1)S(1)}, bf16[512,2048]{1,0:T(8,128)(2,1)}, u32[]{:S(2)}) copy-start(bf16[512,2048]{1,0:T(8,128)(2,1)} %reshape.92) | copy-start | bytes 6291460
  194.6 6.5 %copy-start.6 = (f32[16,8]{0,1:T(8,128)S(1)}, f32[16,8]{0,1:T(8,128)}, u32[]{:S(2)}) copy-start(f32[16,8]{0,1:T(8,128)} %param.22) | copy-start | bytes 1540
  194.6 57.6 %all-to-all-start.1 = ((bf16[128,4,2048]{2,1,0:T(4,128)(2,1)}), bf16[128,4,2048]{2,1,0:T(4,128)(2,1)S(1)}, u32[]{:S(2)}, u32[]{:S(2)}) async-start(bf16[128,4,2048]{2,1,0:T(4,128)(2,1)} %reshape.93), calls=%async_computation.2 | async-start | bytes 4194304 | tf_op jit(solution)/shard_map/all_to_all | solution.py:126
  257.9 5.2 %collective-permute-start.1 = (f32[16,2048]{1,0:T(8,128)S(1)}, f32[16,2048]{1,0:T(8,128)S(1)}, u32[]{:S(2)}, u32[]{:S(2)}) collective-permute-start(f32[16,2048]{1,0:T(8,128)S(1)} %fusion.82), channel_id=1, source_target_pairs={{0,128},{128,0},{1,129},{129,1},{2,130},{130,2},{3,131},{131,3},{4... | collective-permute-start | bytes 393224 | tf_op jit(solution)/shard_map/ppermute | solution.py:139
Sparse Core Ops, SparseCore 0:
  12.7 52.1 all-gather.1
  70.7 35.5 reduce-scatter.1
